TPU v7x, 512 devices: a whole 4x8x8 slice. The times are simulated.
512 devices in a mesh: blk: 64 (over y, z_lo, core), head: 8 (over z_hi, x).
Axes of the slice: x: 4, y: 8, z: 8 (z_hi: 2, z_lo: 4; z = z_hi * 4 + z_lo), core: 2. Of those that a mesh axis runs over, the one named last changes fastest.
Arguments:
- query_rows: bfloat16 [16384, 5120], P(('blk', 'head')), may hold values from -12 to 12
- key_rows: bfloat16 [16384, 1024], P(('blk', 'head')), may hold values from -6 to 6
- value_rows: bfloat16 [16384, 1024], P(('blk', 'head')), may hold values from -6 to 6
- out_grads: bfloat16 [16384, 5120], P(('blk', 'head')), may hold values from -1.75 to 1.75
- lengths: int32 [128], replicated, may hold values from 1 to 128, as said below
- ancestors: int32 [128, 5], replicated, may hold values from -1 to 126, as said below
Outputs:
- query_grads: bfloat16 [16384, 5120], P(('blk', 'head'))
- key_grads: bfloat16 [16384, 1024], P(('blk', 'head'))
- value_grads: bfloat16 [16384, 1024], P(('blk', 'head'))
Inputs may be any that keep to these rules, and one draw needn't show every extreme that they name: `ancestors`: row t lists, in increasing order and followed by -1 entries, the tiles above tile t in the trie other than the 1 prompt tiles, which form a chain above every other tile. Every listed tile is a non-prompt tile below t that lies on the device of tile t or on one of the 2 devices before it; the last listed tile is the parent of t, and the row of a listed tile is a prefix of row t. Rows of prompt tiles are all -1. Some row has no -1 entry. On the devices before the last 3, the last tile of each device not a multiple of 3 has as parent the last tile of the device before, and the second-to-last tile of each device d >= 2 with d % 3 != 1 has as parent the second-to-last tile of the device before; those of the other devices have no non-prompt ancestor. lengths[t] slots of tile t hold tokens, the rest is padding; tile 0 is full.
All inputs are finite; a program needn't handle non-finite values.
Results may differ from a plain program's by a relative error of at most 0.0052.
Values may be sent and summed in bfloat16 or wider, within the bound.
No kernel may reach another device: no remote copies, remote signals or barrier semaphores. Data moves between devices by JAX's collectives and lax.ppermute only.
A program may use at most 64 MiB of HBM per device.

v0:
```python
import jax
import jax.numpy as jnp
from jax import lax
from jax.sharding import PartitionSpec as P

HD = 128
TILE = 128
SPAN_DEV = 2
PROMPT_TILES = 1
ANC = 5
KEYT = 7


def spread(value, axis, source):
    kept = jnp.where(lax.axis_index(axis) == source, value, 0).astype(value.dtype)
    return lax.psum(kept, axis)


def passed_along(block, axis, distance):
    devices = range(lax.axis_size(axis))
    route = [(i - distance, i) for i in devices if i - distance in devices]
    return lax.ppermute(block, axis, route)


def visible_mask(tile_id, tile_ids, listed, lengths):
    position = jnp.arange(TILE, dtype=jnp.int32)
    slot_ok = jnp.concatenate(
        [jnp.arange(PROMPT_TILES, dtype=jnp.int32) < tile_id, listed >= 0, jnp.ones((1,), bool)]
    )
    key_len = jnp.take(lengths, jnp.maximum(tile_ids, 0))
    key_ok = slot_ok[:, None] & (position[None, :] < key_len[:, None])
    own_slot = jnp.arange(KEYT) == KEYT - 1
    causal = position[None, None, :] <= position[:, None, None]
    allowed = key_ok[None, :, :] & (causal | ~own_slot[None, :, None])
    return allowed.reshape(TILE, KEYT * TILE)


def tile_backward(queries, grads_out, key_block, value_block, allowed, live_rows, scaling):
    scores = (
        jnp.einsum("igrd,jgd->grij", queries, key_block, preferred_element_type=jnp.float32)
        * scaling
    )
    scores = jnp.where(allowed, scores, -jnp.inf)
    row_max = jnp.max(scores, axis=-1, keepdims=True)
    log_total = row_max + jnp.log(jnp.sum(jnp.exp(scores - row_max), axis=-1, keepdims=True))
    weights = jnp.where(allowed & live_rows[:, None], jnp.exp(scores - log_total), 0.0)
    weight_grads = jnp.einsum(
        "igrd,jgd->grij", grads_out, value_block, preferred_element_type=jnp.float32
    )
    row_dot = jnp.sum(weights * weight_grads, axis=-1, keepdims=True)
    score_grads = (weights * (weight_grads - row_dot)).astype(jnp.bfloat16)
    weights_low = weights.astype(jnp.bfloat16)
    query_part = (
        jnp.einsum("grij,jgd->igrd", score_grads, key_block, preferred_element_type=jnp.float32)
        * scaling
    )
    key_part = jnp.einsum(
        "grij,igrd->jgd", score_grads, queries, preferred_element_type=jnp.float32
    )
    value_part = jnp.einsum(
        "grij,igrd->jgd", weights_low, grads_out, preferred_element_type=jnp.float32
    )
    return (query_part.astype(jnp.bfloat16), key_part, value_part)


def shards(query_rows, key_rows, value_rows, out_grads, lengths, ancestors):
    head_query, head_key, head_value, head_grad = (
        lax.all_to_all(query_rows, "head", split_axis=1, concat_axis=0, tiled=True),
        lax.all_to_all(key_rows, "head", split_axis=1, concat_axis=0, tiled=True),
        lax.all_to_all(value_rows, "head", split_axis=1, concat_axis=0, tiled=True),
        lax.all_to_all(out_grads, "head", split_axis=1, concat_axis=0, tiled=True),
    )
    row_count = head_query.shape[0]
    tiles_here = row_count // TILE
    kv_width = head_key.shape[1]
    kv_heads = kv_width // HD
    group_size = head_query.shape[1] // kv_width
    scaling = HD ** (-0.5)
    block_index = lax.axis_index("blk")
    first_tile = block_index * tiles_here
    window_first = (block_index - SPAN_DEV) * tiles_here
    window_slots = (SPAN_DEV + 1) * tiles_here
    own_states = jnp.concatenate(
        [
            head_key.reshape(tiles_here, TILE, kv_width),
            head_value.reshape(tiles_here, TILE, kv_width),
        ],
        axis=2,
    )
    my_lists = lax.dynamic_slice_in_dim(ancestors, first_tile, tiles_here, 0)
    prompt_ids = jnp.arange(PROMPT_TILES, dtype=jnp.int32)
    pieces = [spread(own_states[:PROMPT_TILES], "blk", 0)]
    for offset in range(SPAN_DEV, 0, -1):
        pieces.append(passed_along(own_states, "blk", offset))
    pieces.append(own_states)
    table = jnp.concatenate(pieces, axis=0)
    slot_index = jnp.arange(window_slots, dtype=jnp.int32)
    prompt_sum = jnp.zeros((PROMPT_TILES, TILE, 2 * kv_width), jnp.float32)
    near_sum = jnp.zeros((window_slots, TILE * 2 * kv_width), jnp.float32)
    query_parts = []
    for local in range(tiles_here):
        tile_id = first_tile + local
        listed = my_lists[local]
        tile_ids = jnp.concatenate([prompt_ids, listed, tile_id[None]])
        near_rows = jnp.where(listed >= 0, PROMPT_TILES + listed - window_first, 0)
        own_row = jnp.full((1,), PROMPT_TILES + SPAN_DEV * tiles_here + local, jnp.int32)
        table_rows = jnp.concatenate([prompt_ids, near_rows, own_row])
        chosen = jnp.take(table, table_rows, axis=0)
        key_block = chosen[:, :, :kv_width].reshape(KEYT * TILE, kv_heads, HD)
        value_block = chosen[:, :, kv_width:].reshape(KEYT * TILE, kv_heads, HD)
        allowed = visible_mask(tile_id, tile_ids, listed, lengths)
        live_rows = jnp.arange(TILE, dtype=jnp.int32) < lengths[tile_id]
        tile_query = head_query[local * TILE : (local + 1) * TILE].reshape(
            TILE, kv_heads, group_size, HD
        )
        tile_grad = head_grad[local * TILE : (local + 1) * TILE].reshape(
            TILE, kv_heads, group_size, HD
        )
        query_part, key_part, value_part = tile_backward(
            tile_query, tile_grad, key_block, value_block, allowed, live_rows, scaling
        )
        query_parts.append(query_part.reshape(TILE, group_size * kv_width))
        tile_terms = jnp.concatenate(
            [key_part.reshape(KEYT, TILE, kv_width), value_part.reshape(KEYT, TILE, kv_width)],
            axis=2,
        )
        prompt_sum = prompt_sum + tile_terms[:PROMPT_TILES]
        window_ids = jnp.concatenate(
            [listed - window_first, jnp.full((1,), SPAN_DEV * tiles_here + local, jnp.int32)]
        )
        usable = jnp.concatenate([listed >= 0, jnp.ones((1,), bool)])
        placing = ((window_ids[:, None] == slot_index[None, :]) & usable[:, None]).astype(
            jnp.float32
        )
        near_sum = near_sum + jnp.einsum(
            "sw,sx->wx",
            placing,
            tile_terms[PROMPT_TILES:].reshape(ANC + 1, TILE * 2 * kv_width),
            precision=lax.Precision.HIGHEST,
        )
    root_total = lax.psum(prompt_sum, "blk")
    near_parts = near_sum.reshape(SPAN_DEV + 1, tiles_here, TILE, 2 * kv_width)
    total = near_parts[SPAN_DEV]
    for offset in range(1, SPAN_DEV + 1):
        total = total + passed_along(near_parts[SPAN_DEV - offset], "blk", -offset)
    total = total.at[:PROMPT_TILES].add(jnp.where(block_index == 0, root_total, 0.0))
    key_out = (total[:, :, :kv_width] * scaling).astype(jnp.bfloat16).reshape(row_count, kv_width)
    value_out = total[:, :, kv_width:].astype(jnp.bfloat16).reshape(row_count, kv_width)
    query_out = jnp.concatenate(query_parts, axis=0)
    query_grads, key_grads, value_grads = (
        lax.all_to_all(query_out, "head", split_axis=0, concat_axis=1, tiled=True),
        lax.all_to_all(key_out, "head", split_axis=0, concat_axis=1, tiled=True),
        lax.all_to_all(value_out, "head", split_axis=0, concat_axis=1, tiled=True),
    )
    return (query_grads, key_grads, value_grads)


def solution(mesh):
    placed = (
        P(("blk", "head"), None),
        P(("blk", "head"), None),
        P(("blk", "head"), None),
        P(("blk", "head"), None),
        P(),
        P(),
    )
    return jax.shard_map(
        shards,
        mesh=mesh,
        in_specs=placed,
        out_specs=(P(("blk", "head"), None), P(("blk", "head"), None), P(("blk", "head"), None)),
        check_vma=False,
    )
```

profile of v0, /device:TPU:2, one launch (start us, length us, event | category | flops | bytes accessed | tf_op | source)
XLA Modules:
  0.0 1101.3 jit_solution(1257224561000166744)
XLA Ops:
  7.2 0.8 copy-done
  8.0 0.6 copy_bitcast_fusion.7
  8.7 13.3 %all-to-all-start = ((bf16[32,8,128]{2,0,1:T(8,128)(2,1)}), bf16[32,8,128]{2,0,1:T(8,128)(2,1)S(1)}, u32[]{:S(2)}, u32[]{:S(2)}) async-start(bf16[32,8,128]{2,0,1:T(8,128)(2,1)} %copy_bitcast_fusion.7), calls=%async_computation | async-start | bytes 131072 | tf_op jit(solution)/shard_map/all_to_all | solution.py:69
  21.9 0.8 constant_dynamic-slice_fusion
  23.3 1.4 fusion.74
  24.7 1.3 gather_fusion.3
  26.1 1.3 gather_fusion.1
  27.5 1.5 copy_bitcast_fusion.6
  29.0 1.3 iota_compare_fusion.3
  30.7 9.6 all-to-all-start.1
  40.4 1.7 copy.149
  42.1 0.7 copy.148
  43.3 5.8 all-to-all-done.1
  49.1 4.8 all-to-all-start.2
  53.9 3.6 collective-permute-start
  57.5 1.3 collective-permute-start.1
  58.8 0.6 fusion.43
  59.6 472.7 %all-reduce.3.cloned.1.call-done = bf16[1,128,256]{2,1,0:T(8,128)(2,1)} async-done(((bf16[1,128,256]{2,1,0:T(8,128)(2,1)}), bf16[1,128,256]{2,1,0:T(8,128)(2,1)}) %all-reduce.3.cloned.1.call-update) | async-done | bytes 65552 | tf_op jit(solution)/shard_map/psum | solution.py:16
  532.2 0.9 maximum_maximum_fusion
  534.5 10.4 all-to-all-start.3
  545.4 9.0 all-to-all-done.3
  555.6 0.7 fusion.14
  556.4 1.0 fusion.3
  557.3 0.7 fusion.10
  561.1 0.7 fusion.12
  561.8 0.9 fusion
  562.8 0.7 fusion.11
  564.5 0.8 fusion.45
  565.3 0.8 convolution_add_fusion
  566.5 1.3 collective-permute-start.2
  567.8 1.3 collective-permute-start.3
  569.6 0.7 fusion.26
  570.3 8.4 collective-permute-done.3
  578.8 1.1 fusion.24
  579.9 465.2 %all-reduce.5.cloned.1.call-done = f32[1,128,256]{2,1,0:T(8,128)} async-done(((f32[1,128,256]{2,1,0:T(8,128)}), f32[1,128,256]{2,1,0:T(8,128)}) %all-reduce.5.cloned.1.call-update) | async-done | bytes 131088 | tf_op jit(solution)/shard_map/psum | solution.py:141
  1045.1 0.9 fusion.27
  1046.1 0.6 slice.174
  1046.7 10.3 all-to-all-start.6
  1057.0 0.6 fusion.25
  1057.7 8.2 all-to-all-done.6
  1065.8 4.7 all-to-all-start.5
  1070.6 0.8 pad_maximum_fusion
  1071.3 8.1 all-to-all-done.5
  1079.4 4.8 all-to-all-start.4
  1084.2 0.6 copy_bitcast_fusion.4
  1084.8 0.6 copy_bitcast_fusion.5
  1085.4 8.3 all-to-all-done.4
  1093.7 0.8 copy.107
  (70 shorter events, 9.7 us)
Async XLA Ops:
  7.2 0.8 copy-start
  8.0 34.1 %copy-start.1 = (bf16[32,5120]{1,0:T(8,128)(2,1)S(1)}, bf16[32,5120]{1,0:T(8,128)(2,1)}, u32[]{:S(2)}) copy-start(bf16[32,5120]{1,0:T(8,128)(2,1)} %param.15) | copy-start | bytes 983044
  8.7 22.1 %all-to-all-start = ((bf16[32,8,128]{2,0,1:T(8,128)(2,1)}), bf16[32,8,128]{2,0,1:T(8,128)(2,1)S(1)}, u32[]{:S(2)}, u32[]{:S(2)}) async-start(bf16[32,8,128]{2,0,1:T(8,128)(2,1)} %copy_bitcast_fusion.7), calls=%async_computation | async-start | bytes 131072 | tf_op jit(solution)/shard_map/all_to_all | solution.py:69
  30.7 18.4 %all-to-all-start.1 = ((bf16[32,8,128]{2,0,1:T(8,128)(2,1)}), bf16[32,8,128]{2,0,1:T(8,128)(2,1)S(1)}, u32[]{:S(2)}, u32[]{:S(2)}) async-start(bf16[32,8,128]{2,0,1:T(8,128)(2,1)} %copy_bitcast_fusion.6), calls=%async_computation.1 | async-start | bytes 131072 | tf_op jit(solution)/shard_map/all_to_all | solution.py:70
  49.1 485.4 %all-to-all-start.2 = ((bf16[32,8,640]{2,0,1:T(8,128)(2,1)}), bf16[32,8,640]{2,0,1:T(8,128)(2,1)S(1)}, u32[]{:S(2)}, u32[]{:S(2)}) async-start(bf16[32,8,640]{2,0,1:T(8,128)(2,1)} %bitcast.235), calls=%async_computation.2 | async-start | bytes 655360 | tf_op jit(solution)/shard_map/all_to_all | solution.py:68
  53.9 478.3 %all-reduce.3.cloned.1.call-start = ((), (), s32[]{:S(2)}) async-start(), calls=%async_computation.7 | async-start | bytes 131072 | tf_op jit(solution)/shard_map/psum | solution.py:16
  53.9 478.3 %collective-permute-start = (bf16[2,128,256]{2,1,0:T(8,128)(2,1)S(1)}, bf16[2,128,256]{2,1,0:T(8,128)(2,1)S(1)}, u32[]{:S(2)}, u32[]{:S(2)}) collective-permute-start(bf16[2,128,256]{2,1,0:T(8,128)(2,1)S(1)} %pad_maximum_fusion.1), channel_id=1, source_target_pairs={{0,16},{8,24},{16,32},{24,40},{32,48},{40,56},{48,64},{56,72},{64,... | collective-permute-start | bytes 393224 | tf_op jit(solution)/shard_map/ppermute | solution.py:22
  57.5 474.7 %collective-permute-start.1 = (bf16[2,128,256]{2,1,0:T(8,128)(2,1)S(1)}, bf16[2,128,256]{2,1,0:T(8,128)(2,1)S(1)}, u32[]{:S(2)}, u32[]{:S(2)}) collective-permute-start(bf16[2,128,256]{2,1,0:T(8,128)(2,1)S(1)} %pad_maximum_fusion.1), channel_id=1, source_target_pairs={{0,8},{8,16},{16,24},{24,32},{32,40},{40,48},{48,56},{56,64},{64,7... | collective-permute-start | bytes 393224 | tf_op jit(solution)/shard_map/ppermute | solution.py:22
  534.5 19.9 %all-to-all-start.3 = ((bf16[32,8,640]{2,0,1:T(8,128)(2,1)}), bf16[32,8,640]{2,0,1:T(8,128)(2,1)S(1)}, u32[]{:S(2)}, u32[]{:S(2)}) async-start(bf16[32,8,640]{2,0,1:T(8,128)(2,1)} %bitcast.234), calls=%async_computation.3 | async-start | bytes 655360 | tf_op jit(solution)/shard_map/all_to_all | solution.py:71
  544.9 500.2 %all-reduce.5.cloned.1.call-start = ((), (), s32[]{:S(2)}) async-start(), calls=%async_computation.8 | async-start | bytes 262144 | tf_op jit(solution)/shard_map/psum | solution.py:141
  566.5 3.9 collective-permute-start.2
  567.8 11.0 %collective-permute-start.3 = (f32[2,128,256]{2,1,0:T(8,128)S(1)}, f32[2,128,256]{2,1,0:T(8,128)}, u32[]{:S(2)}, u32[]{:S(2)}) collective-permute-start(f32[2,128,256]{2,1,0:T(8,128)S(1)} %bitcast.269), channel_id=1, source_target_pairs={{16,0},{24,8},{32,16},{40,24},{48,32},{56,40},{64,48},{72,56},{80,... | collective-permute-start | bytes 786440 | tf_op jit(solution)/shard_map/ppermute | solution.py:22
  1046.7 19.1 %all-to-all-start.6 = ((bf16[8,32,128]{2,1,0:T(8,128)(2,1)}), bf16[8,32,128]{2,1,0:T(8,128)(2,1)S(1)}, u32[]{:S(2)}, u32[]{:S(2)}) async-start(bf16[8,32,128]{2,1,0:T(8,128)(2,1)} %bitcast.69), calls=%async_computation.6 | async-start | bytes 131072 | tf_op jit(solution)/shard_map/all_to_all | solution.py:153
  1065.8 13.6 %all-to-all-start.5 = ((bf16[8,32,128]{2,1,0:T(8,128)(2,1)}), bf16[8,32,128]{2,1,0:T(8,128)(2,1)S(1)}, u32[]{:S(2)}, u32[]{:S(2)}) async-start(bf16[8,32,128]{2,1,0:T(8,128)(2,1)} %bitcast.67), calls=%async_computation.5 | async-start | bytes 131072 | tf_op jit(solution)/shard_map/all_to_all | solution.py:152
  1079.4 14.3 %all-to-all-start.4 = ((bf16[8,32,640]{2,1,0:T(8,128)(2,1)}), bf16[8,32,640]{2,1,0:T(8,128)(2,1)S(1)}, u32[]{:S(2)}, u32[]{:S(2)}) async-start(bf16[8,32,640]{2,1,0:T(8,128)(2,1)} %bitcast.43), calls=%async_computation.4 | async-start | bytes 655360 | tf_op jit(solution)/shard_map/all_to_all | solution.py:151
Sparse Core Ops, SparseCore 0:
  59.6 472.5 all-reduce.2
  570.5 474.6 all-reduce.4
where the time goes:
time: 1100 us
  waiting for transfers between devices  986 us (90%)
  starting transfers between devices  65.3 us (6%)
  local copies, waits for them, and re-layouts  17.1 us (2%)
  between operations  14.5 us (1%)
  other arithmetic  11 us (1%)
    psum x1, waiting for transfers between devices, spread(): return lax.psum(kept, axis)  473 us
    psum x1, waiting for transfers between devices, shards(): root_total = lax.psum(prompt_sum, 'blk')  465 us
  transfers between devices with their start and end apart: 13, of which 9 were waited for; matrix products, arithmetic and copies ran while one was open for 2% of the time, Pallas kernels for 0%

commit v1 on v0

--- a/solution.py
+++ b/solution.py
@@ -13,7 +13,7 @@
 
 def spread(value, axis, source):
     kept = jnp.where(lax.axis_index(axis) == source, value, 0).astype(value.dtype)
-    return lax.psum(kept, axis)
+    return jnp.sum(lax.all_gather(kept, axis), axis=0)
 
 
 def passed_along(block, axis, distance):

time: 1100 us -> 725 us (0.66)
  waiting for transfers between devices: 986 us -> 618 us
    psum x1 -> x0, waiting for transfers between devices: 473 us -> none  [spread(): return lax.psum(kept, axis)]
    all_gather x0 -> x1, waiting for transfers between devices: none -> 87.4 us  [spread(): return jnp.sum(lax.all_gather(kept, axis), axis=0)]
  transfers between devices with their start and end apart: 13 -> 13, of which waited for: 9 -> 10; matrix products, arithmetic and copies ran while one was open for 2% -> 3% of each run, Pallas kernels for 0% -> 0%
where the time goes in v1:
time: 725 us; the launch traced here: 724 us
  waiting for transfers between devices  618 us (85%)
  starting transfers between devices  56.2 us (8%)
  local copies, waits for them, and re-layouts  14.9 us (2%)
  between operations  14.5 us (2%)
  other arithmetic  12.9 us (2%)
  matrix products  7.66 us (1%)
    psum x1, waiting for transfers between devices, shards(): root_total = lax.psum(prompt_sum, 'blk')  468 us
    all_gather x1, waiting for transfers between devices, spread(): return jnp.sum(lax.all_gather(kept, axis), axis=0)  87.4 us
  transfers between devices with their start and end apart: 13, of which 10 were waited for; matrix products, arithmetic and copies ran while one was open for 3% of the time, Pallas kernels for 0%

profile of v1, /device:TPU:2, one launch (start us, length us, event | category | flops | bytes accessed | tf_op | source)
XLA Modules:
  0.0 724.0 jit_solution(4226015968503339106)
XLA Ops:
  7.2 0.8 copy-done
  8.0 0.6 copy_bitcast_fusion.7
  8.7 13.3 %all-to-all-start = ((bf16[32,8,128]{2,0,1:T(8,128)(2,1)}), bf16[32,8,128]{2,0,1:T(8,128)(2,1)S(1)}, u32[]{:S(2)}, u32[]{:S(2)}) async-start(bf16[32,8,128]{2,0,1:T(8,128)(2,1)} %copy_bitcast_fusion.7), calls=%async_computation | async-start | bytes 131072 | tf_op jit(solution)/shard_map/all_to_all | solution.py:69
  21.9 1.5 copy_bitcast_fusion.6
  23.4 7.3 %all-to-all-done = bf16[32,8,128]{2,0,1:T(8,128)(2,1)S(1)} async-done(((bf16[32,8,128]{2,0,1:T(8,128)(2,1)}), bf16[32,8,128]{2,0,1:T(8,128)(2,1)S(1)}, u32[]{:S(2)}, u32[]{:S(2)}) %all-to-all-start) | async-done | bytes 65568 | tf_op jit(solution)/shard_map/all_to_all | solution.py:69
  30.7 4.7 all-to-all-start.1
  35.5 8.8 %all-to-all-done.1 = bf16[32,8,128]{2,0,1:T(8,128)(2,1)S(1)} async-done(((bf16[32,8,128]{2,0,1:T(8,128)(2,1)}), bf16[32,8,128]{2,0,1:T(8,128)(2,1)S(1)}, u32[]{:S(2)}, u32[]{:S(2)}) %all-to-all-start.1) | async-done | bytes 65568 | tf_op jit(solution)/shard_map/all_to_all | solution.py:70
  44.3 0.6 fusion.43
  45.0 1.7 copy.149
  46.7 4.8 all-to-all-start.2
  51.5 0.8 constant_dynamic-slice_fusion
  52.5 0.6 gather_fusion.3
  53.2 0.6 gather_fusion.1
  54.7 1.2 iota_compare_fusion.3
  56.4 0.7 copy.148
  57.8 3.3 all-to-all-done.2
  61.1 6.4 all-to-all-start.3
  67.5 3.4 collective-permute-start
  70.9 1.3 collective-permute-start.1
  72.7 8.2 %all-to-all-done.3 = bf16[32,8,640]{2,0,1:T(8,128)(2,1)S(1)} async-done(((bf16[32,8,640]{2,0,1:T(8,128)(2,1)}), bf16[32,8,640]{2,0,1:T(8,128)(2,1)S(1)}, u32[]{:S(2)}, u32[]{:S(2)}) %all-to-all-start.3) | async-done | bytes 327712 | tf_op jit(solution)/shard_map/all_to_all | solution.py:71
  81.4 87.4 %all-gather.3.cloned.1.call-done = bf16[64,128,256]{2,1,0:T(8,128)(2,1)} async-done(((bf16[1,128,256]{2,1,0:T(8,128)(2,1)}), bf16[64,128,256]{2,1,0:T(8,128)(2,1)}) %all-gather.3.cloned.1.call-update) | async-done | bytes 4194320 | tf_op jit(solution)/shard_map/all_gather | solution.py:16
  168.8 2.8 reduce.10
  173.4 0.7 fusion.14
  174.1 1.0 fusion.3
  175.1 0.7 fusion.10
  179.3 0.7 fusion.12
  180.0 0.9 fusion
  180.9 0.7 fusion.11
  182.7 0.8 fusion.45
  183.5 0.8 convolution_add_fusion
  184.7 1.3 collective-permute-start.2
  186.0 1.3 collective-permute-start.3
  187.8 0.7 fusion.26
  188.5 9.9 %collective-permute-done.3 = f32[2,128,256]{2,1,0:T(8,128)} collective-permute-done((f32[2,128,256]{2,1,0:T(8,128)S(1)}, f32[2,128,256]{2,1,0:T(8,128)}, u32[]{:S(2)}, u32[]{:S(2)}) %collective-permute-start.3) | collective-permute-done | bytes 262176 | tf_op jit(solution)/shard_map/ppermute | solution.py:22
  198.5 1.1 fusion.24
  199.5 468.3 %all-reduce.2.cloned.1.call-done = f32[1,128,256]{2,1,0:T(8,128)} async-done(((f32[1,128,256]{2,1,0:T(8,128)}), f32[1,128,256]{2,1,0:T(8,128)}) %all-reduce.2.cloned.1.call-update) | async-done | bytes 131088 | tf_op jit(solution)/shard_map/psum | solution.py:141
  667.8 0.9 fusion.27
  668.8 0.6 slice.174
  669.4 10.3 %all-to-all-start.6 = ((bf16[8,32,128]{2,1,0:T(8,128)(2,1)}), bf16[8,32,128]{2,1,0:T(8,128)(2,1)S(1)}, u32[]{:S(2)}, u32[]{:S(2)}) async-start(bf16[8,32,128]{2,1,0:T(8,128)(2,1)} %bitcast.70), calls=%async_computation.6 | async-start | bytes 131072 | tf_op jit(solution)/shard_map/all_to_all | solution.py:153
  679.8 0.6 fusion.25
  680.4 8.2 %all-to-all-done.6 = bf16[8,32,128]{2,1,0:T(8,128)(2,1)S(1)} async-done(((bf16[8,32,128]{2,1,0:T(8,128)(2,1)}), bf16[8,32,128]{2,1,0:T(8,128)(2,1)S(1)}, u32[]{:S(2)}, u32[]{:S(2)}) %all-to-all-start.6) | async-done | bytes 65568 | tf_op jit(solution)/shard_map/all_to_all | solution.py:153
  688.6 4.7 all-to-all-start.5
  693.3 0.8 pad_maximum_fusion
  694.0 8.1 %all-to-all-done.5 = bf16[8,32,128]{2,1,0:T(8,128)(2,1)S(1)} async-done(((bf16[8,32,128]{2,1,0:T(8,128)(2,1)}), bf16[8,32,128]{2,1,0:T(8,128)(2,1)S(1)}, u32[]{:S(2)}, u32[]{:S(2)}) %all-to-all-start.5) | async-done | bytes 65568 | tf_op jit(solution)/shard_map/all_to_all | solution.py:152
  702.1 4.8 all-to-all-start.4
  706.9 0.6 copy_bitcast_fusion.4
  708.2 8.3 %all-to-all-done.4 = bf16[8,32,640]{2,1,0:T(8,128)(2,1)S(1)} async-done(((bf16[8,32,640]{2,1,0:T(8,128)(2,1)}), bf16[8,32,640]{2,1,0:T(8,128)(2,1)S(1)}, u32[]{:S(2)}, u32[]{:S(2)}) %all-to-all-start.4) | async-done | bytes 327712 | tf_op jit(solution)/shard_map/all_to_all | solution.py:151
  716.4 0.8 copy.107
  (73 shorter events, 10.8 us)
Async XLA Ops:
  7.2 0.8 copy-start
  7.2 45.3 %copy-start.1 = (s32[128]{0:T(128)S(1)}, s32[128]{0:T(128)}, u32[]{:S(2)}) copy-start(s32[128]{0:T(128)} %param.16) | copy-start | bytes 1540
  8.0 48.4 %copy-start.2 = (bf16[32,5120]{1,0:T(8,128)(2,1)S(1)}, bf16[32,5120]{1,0:T(8,128)(2,1)}, u32[]{:S(2)}) copy-start(bf16[32,5120]{1,0:T(8,128)(2,1)} %param.15) | copy-start | bytes 983044
  8.7 22.1 %all-to-all-start = ((bf16[32,8,128]{2,0,1:T(8,128)(2,1)}), bf16[32,8,128]{2,0,1:T(8,128)(2,1)S(1)}, u32[]{:S(2)}, u32[]{:S(2)}) async-start(bf16[32,8,128]{2,0,1:T(8,128)(2,1)} %copy_bitcast_fusion.7), calls=%async_computation | async-start | bytes 131072 | tf_op jit(solution)/shard_map/all_to_all | solution.py:69
  30.7 13.6 %all-to-all-start.1 = ((bf16[32,8,128]{2,0,1:T(8,128)(2,1)}), bf16[32,8,128]{2,0,1:T(8,128)(2,1)S(1)}, u32[]{:S(2)}, u32[]{:S(2)}) async-start(bf16[32,8,128]{2,0,1:T(8,128)(2,1)} %copy_bitcast_fusion.6), calls=%async_computation.1 | async-start | bytes 131072 | tf_op jit(solution)/shard_map/all_to_all | solution.py:70
  35.5 133.3 %all-gather.3.cloned.1.call-start = ((), (), s32[]{:S(2)}) async-start(), calls=%async_computation.8 | async-start | bytes 4259840 | tf_op jit(solution)/shard_map/all_gather | solution.py:16
  46.7 14.4 %all-to-all-start.2 = ((bf16[32,8,640]{2,0,1:T(8,128)(2,1)}), bf16[32,8,640]{2,0,1:T(8,128)(2,1)S(1)}, u32[]{:S(2)}, u32[]{:S(2)}) async-start(bf16[32,8,640]{2,0,1:T(8,128)(2,1)} %bitcast.236), calls=%async_computation.2 | async-start | bytes 655360 | tf_op jit(solution)/shard_map/all_to_all | solution.py:68
  61.1 19.8 %all-to-all-start.3 = ((bf16[32,8,640]{2,0,1:T(8,128)(2,1)}), bf16[32,8,640]{2,0,1:T(8,128)(2,1)S(1)}, u32[]{:S(2)}, u32[]{:S(2)}) async-start(bf16[32,8,640]{2,0,1:T(8,128)(2,1)} %bitcast.235), calls=%async_computation.3 | async-start | bytes 655360 | tf_op jit(solution)/shard_map/all_to_all | solution.py:71
  67.4 600.4 %all-reduce.2.cloned.1.call-start = ((), (), s32[]{:S(2)}) async-start(), calls=%async_computation.7 | async-start | bytes 262144 | tf_op jit(solution)/shard_map/psum | solution.py:141
  67.5 104.0 %collective-permute-start = (bf16[2,128,256]{2,1,0:T(8,128)(2,1)S(1)}, bf16[2,128,256]{2,1,0:T(8,128)(2,1)S(1)}, u32[]{:S(2)}, u32[]{:S(2)}) collective-permute-start(bf16[2,128,256]{2,1,0:T(8,128)(2,1)S(1)} %pad_maximum_fusion.1), channel_id=1, source_target_pairs={{0,16},{8,24},{16,32},{24,40},{32,48},{40,56},{48,64},{56,72},{64,... | collective-permute-start | bytes 393224 | tf_op jit(solution)/shard_map/ppermute | solution.py:22
  70.9 100.6 %collective-permute-start.1 = (bf16[2,128,256]{2,1,0:T(8,128)(2,1)S(1)}, bf16[2,128,256]{2,1,0:T(8,128)(2,1)S(1)}, u32[]{:S(2)}, u32[]{:S(2)}) collective-permute-start(bf16[2,128,256]{2,1,0:T(8,128)(2,1)S(1)} %pad_maximum_fusion.1), channel_id=1, source_target_pairs={{0,8},{8,16},{16,24},{24,32},{32,40},{40,48},{48,56},{56,64},{64,7... | collective-permute-start | bytes 393224 | tf_op jit(solution)/shard_map/ppermute | solution.py:22
  184.7 3.9 collective-permute-start.2
  186.0 12.5 %collective-permute-start.3 = (f32[2,128,256]{2,1,0:T(8,128)S(1)}, f32[2,128,256]{2,1,0:T(8,128)}, u32[]{:S(2)}, u32[]{:S(2)}) collective-permute-start(f32[2,128,256]{2,1,0:T(8,128)S(1)} %bitcast.271), channel_id=1, source_target_pairs={{16,0},{24,8},{32,16},{40,24},{48,32},{56,40},{64,48},{72,56},{80,... | collective-permute-start | bytes 786440 | tf_op jit(solution)/shard_map/ppermute | solution.py:22
  669.4 19.1 %all-to-all-start.6 = ((bf16[8,32,128]{2,1,0:T(8,128)(2,1)}), bf16[8,32,128]{2,1,0:T(8,128)(2,1)S(1)}, u32[]{:S(2)}, u32[]{:S(2)}) async-start(bf16[8,32,128]{2,1,0:T(8,128)(2,1)} %bitcast.70), calls=%async_computation.6 | async-start | bytes 131072 | tf_op jit(solution)/shard_map/all_to_all | solution.py:153
  688.6 13.6 %all-to-all-start.5 = ((bf16[8,32,128]{2,1,0:T(8,128)(2,1)}), bf16[8,32,128]{2,1,0:T(8,128)(2,1)S(1)}, u32[]{:S(2)}, u32[]{:S(2)}) async-start(bf16[8,32,128]{2,1,0:T(8,128)(2,1)} %bitcast.68), calls=%async_computation.5 | async-start | bytes 131072 | tf_op jit(solution)/shard_map/all_to_all | solution.py:152
  702.1 14.3 %all-to-all-start.4 = ((bf16[8,32,640]{2,1,0:T(8,128)(2,1)}), bf16[8,32,640]{2,1,0:T(8,128)(2,1)S(1)}, u32[]{:S(2)}, u32[]{:S(2)}) async-start(bf16[8,32,640]{2,1,0:T(8,128)(2,1)} %bitcast.44), calls=%async_computation.4 | async-start | bytes 655360 | tf_op jit(solution)/shard_map/all_to_all | solution.py:151
Sparse Core Ops, SparseCore 0:
  45.1 123.6 all-gather.2
  188.6 479.1 all-reduce.1
